TPU v7x, 512 devices: a whole 4x4x16 slice. The times are simulated.
512 devices in a mesh: chan: 32 (over z, x_hi), seg: 16 (over y, x_lo, core).
Axes of the slice: x: 4 (x_hi: 2, x_lo: 2; x = x_hi * 2 + x_lo), y: 4, z: 16, core: 2. Of those that a mesh axis runs over, the one named last changes fastest.
Arguments:
- traces: bfloat16 [512, 16, 384], P('chan', 'seg')
- taper_len: int32 [512], P('chan'), may hold values from 1 to 192
- gather_id: int32 [512, 512], P('chan'), may hold values from 0 to 511, as said below
- offset_bin: int32 [512, 512], P('chan'), may hold values from 0 to 1, as said below
Outputs:
- stack: float32 [512, 2, 256], P(('chan', 'seg'))
Inputs may be any that keep to these rules, and one draw needn't show every extreme that they name: Channels lie on a fiber at integer positions p_0 < p_1 < ... with steps of 2 to 5; gather_id[i, j] = floor((p_i + p_j - 2 p_0) * 512 / (2 (p_last - p_0) + 1)). offset_bin[i, j] = floor(|p_i - p_j| * 2 / (p_last - p_0 + 1)) with the same positions.
All inputs are finite; a program needn't handle non-finite values.
Results may differ from a plain program's by a relative error of at most 0.0039.
Values may be sent and summed in bfloat16 or wider, within the bound.
No kernel may reach another device: no remote copies, remote signals or barrier semaphores. Data moves between devices by JAX's collectives and lax.ppermute only.
A program may use at most 64 MiB of HBM per device.

v0:
```python
import math
import jax
import jax.numpy as jnp
from jax import lax
from jax.sharding import PartitionSpec as P

LAGS = 256
OFFBINS = 2


def normalize(traces, taper_len):
    values = traces.astype(jnp.float32)
    sample_count = values.shape[2]
    power = jnp.mean(values * values, axis=2, keepdims=True)
    times = jnp.arange(sample_count).astype(jnp.float32)
    length = taper_len.astype(jnp.float32)[:, None, None]
    window = jnp.minimum(1.0, jnp.minimum((times + 1.0) / length, (sample_count - times) / length))
    return (window * values * lax.rsqrt(power + 1e-06)).astype(jnp.bfloat16)


def hankel(normed, lag_count):
    chan_count, seg_count, sample_count = normed.shape
    turned = jnp.transpose(normed, (1, 2, 0))
    padded = jnp.pad(turned, ((0, 0), (lag_count // 2, lag_count // 2), (0, 0)))
    slices = [padded[:, lag_count - k : lag_count - k + sample_count, :] for k in range(lag_count)]
    picked = jnp.stack(slices, axis=3)
    return picked.reshape(seg_count * sample_count, chan_count * lag_count)


def shards(traces, taper_len, gather_id, offset_bin):
    chan_count = traces.shape[0]
    chan_devices = lax.axis_size("chan")
    seg_devices = lax.axis_size("seg")
    bucket_count = chan_devices * seg_devices * OFFBINS
    normed = normalize(traces, taper_len)
    kernel = hankel(normed, LAGS)
    first_row = lax.axis_index("chan") * chan_count
    own_rows = first_row + jnp.arange(chan_count, dtype=jnp.int32)[None, :]
    empty = jnp.zeros((bucket_count, LAGS), jnp.float32)
    piece = lax.all_gather(normed, "chan", axis=0, tiled=True)
    row_count = piece.shape[0]
    product = jnp.dot(piece.reshape(row_count, -1), kernel, preferred_element_type=jnp.float32)
    product = product.reshape(row_count * chan_count, LAGS)
    labels = jnp.transpose(gather_id * OFFBINS + offset_bin)
    partner = jnp.arange(row_count, dtype=jnp.int32)[:, None]
    labels = jnp.where(partner == own_rows, bucket_count, labels).reshape(-1)
    total = empty.at[labels].add(product, mode="drop")
    scale = 1.0 / math.sqrt(traces.shape[2] * traces.shape[1] * seg_devices)
    stacked = (total * scale).reshape(chan_devices * seg_devices, OFFBINS, LAGS)
    result = lax.psum_scatter(stacked, ("chan", "seg"), scatter_dimension=0, tiled=True)
    return result


def solution(mesh):
    placed = (P("chan", "seg", None), P("chan"), P("chan", None), P("chan", None))
    return jax.shard_map(
        shards,
        mesh=mesh,
        in_specs=placed,
        out_specs=P(("chan", "seg"), None, None),
        check_vma=False,
    )
```

profile of v0, /device:TPU:1, one launch (start us, length us, event | category | flops | bytes accessed | tf_op | source)
XLA Modules:
  0.0 647.5 jit_solution(15832972223417551559)
XLA Ops:
  6.5 0.9 fusion.7
  7.4 0.7 convert_element_type.24
  8.1 0.8 fusion.264
  8.9 0.8 fusion.6
  10.2 0.1 constant_dynamic-update-slice_fusion.248
  10.3 0.1 constant_dynamic-update-slice_fusion.247
  10.4 0.1 constant_dynamic-update-slice_fusion.246
  10.4 0.1 constant_dynamic-update-slice_fusion.245
  10.5 0.1 constant_dynamic-update-slice_fusion.244
  10.6 0.1 constant_dynamic-update-slice_fusion.243
  10.7 0.1 constant_dynamic-update-slice_fusion.242
  10.8 0.1 constant_dynamic-update-slice_fusion.241
  10.8 0.1 constant_dynamic-update-slice_fusion.240
  11.5 0.1 constant_dynamic-update-slice_fusion.232
  11.6 0.1 constant_dynamic-update-slice_fusion.231
  11.7 0.1 constant_dynamic-update-slice_fusion.230
  11.7 0.1 constant_dynamic-update-slice_fusion.229
  11.8 0.1 constant_dynamic-update-slice_fusion.228
  11.9 0.1 constant_dynamic-update-slice_fusion.227
  12.0 0.1 constant_dynamic-update-slice_fusion.226
  12.1 0.1 constant_dynamic-update-slice_fusion.225
  12.1 0.1 constant_dynamic-update-slice_fusion.224
  12.2 0.1 constant_dynamic-update-slice_fusion.223
  12.3 0.1 constant_dynamic-update-slice_fusion.222
  12.4 0.1 constant_dynamic-update-slice_fusion.221
  13.0 0.1 constant_dynamic-update-slice_fusion.213
  13.1 0.1 constant_dynamic-update-slice_fusion.212
  13.2 0.1 constant_dynamic-update-slice_fusion.211
  13.3 0.1 constant_dynamic-update-slice_fusion.210
  13.4 0.1 constant_dynamic-update-slice_fusion.209
  13.5 0.1 constant_dynamic-update-slice_fusion.208
  13.5 0.1 constant_dynamic-update-slice_fusion.207
  13.6 0.1 constant_dynamic-update-slice_fusion.206
  13.7 0.1 constant_dynamic-update-slice_fusion.205
  13.8 0.1 constant_dynamic-update-slice_fusion.204
  13.9 0.1 constant_dynamic-update-slice_fusion.203
  13.9 0.1 constant_dynamic-update-slice_fusion.202
  14.6 0.1 constant_dynamic-update-slice_fusion.194
  14.7 0.1 constant_dynamic-update-slice_fusion.193
  14.8 0.1 constant_dynamic-update-slice_fusion.192
  14.8 0.1 constant_dynamic-update-slice_fusion.191
  14.9 0.1 constant_dynamic-update-slice_fusion.190
  15.0 0.1 constant_dynamic-update-slice_fusion.189
  15.1 0.1 constant_dynamic-update-slice_fusion.188
  15.2 0.1 constant_dynamic-update-slice_fusion.187
  15.2 0.1 constant_dynamic-update-slice_fusion.186
  15.3 0.1 constant_dynamic-update-slice_fusion.185
  15.4 0.1 constant_dynamic-update-slice_fusion.184
  15.5 0.1 constant_dynamic-update-slice_fusion.183
  16.1 0.1 constant_dynamic-update-slice_fusion.175
  16.2 0.1 constant_dynamic-update-slice_fusion.174
  16.3 0.1 constant_dynamic-update-slice_fusion.173
  20.1 0.1 constant_dynamic-update-slice_fusion.127
  30.5 0.8 copy.264
  31.3 71.5 %all_gather.3 = bf16[512,1,384]{2,0,1:T(8,128)(2,1)S(1)} all-gather(bf16[16,1,384]{2,0,1:T(8,128)(2,1)S(1)} %fusion.6), channel_id=1, replica_groups=mesh['chan'=32,'seg'=16] {'chan'}, dimensions={0}, use_global_device_ids=true | all-gather | bytes 405504 | tf_op jit(solution)/shard_map/all_gather | solution.py:40
  102.8 5.6 fusion.2
  108.4 9.3 %reshape.172 = f32[8192,256]{1,0:T(8,128)} reshape(f32[512,4096]{1,0:T(8,128)} %fusion.2) | data formatting | bytes 16777216 | tf_op jit(solution)/shard_map/reshape | solution.py:43
  117.8 0.1 copy.263
  117.9 0.2 reshape.163
  118.1 44.9 %scatter_custom_fusion = f32[1024,256]{1,0:T(8,128)S(1)} fusion(s32[8192]{0:T(1024)S(1)} %bitcast.1034, f32[8192,256]{1,0:T(8,128)} %reshape.172, f32[]{:T(128)} %constant.13.clone.1), kind=kCustom, calls=%fused_computation.258 | custom fusion | flops 2097152 | bytes 1049088 | tf_op jit(solution)/shard_map/scatter-add | solution.py:47
  163.0 0.1 broadcast_multiply_fusion
  163.1 1.7 reshape.167
  164.7 474.7 %all-reduce.4.cloned.1.call-done = f32[512,2,256]{2,1,0:T(2,128)} async-done(((f32[512,2,256]{2,1,0:T(2,128)}), f32[512,2,256]{2,1,0:T(2,128)}) %all-reduce.4.cloned.1.call-update) | async-done | bytes 1048592
  639.4 1.2 constant_dynamic-slice_fusion
  (220 shorter events, 16.8 us)
Async XLA Ops:
  6.5 13.5 %copy-start = (bf16[16,1,384]{2,0,1:T(8,128)(2,1)S(1)}, bf16[16,1,384]{2,0,1:T(8,128)(2,1)}, u32[]{:S(2)}) copy-start(bf16[16,1,384]{2,0,1:T(8,128)(2,1)} %param.4) | copy-start | bytes 36868
  6.5 632.9 %all-reduce.4.cloned.1.call-start = ((), (), s32[]{:S(2)}) async-start(), calls=%async_computation | async-start | bytes 2097152
  108.4 9.3 %copy-start.1 = (s32[16,512]{1,0:T(8,128)S(1)}, s32[16,512]{1,0:T(8,128)}, u32[]{:S(2)}) copy-start(s32[16,512]{1,0:T(8,128)} %param.7) | copy-start | bytes 98308
  108.4 9.3 %copy-start.2 = (s32[16,512]{1,0:T(8,128)S(1)}, s32[16,512]{1,0:T(8,128)}, u32[]{:S(2)}) copy-start(s32[16,512]{1,0:T(8,128)} %param.6) | copy-start | bytes 98308
Sparse Core Ops, SparseCore 0:
  164.9 474.5 all-reduce.3
where the time goes:
time: 648 us
  waiting for transfers between devices  475 us (73%)
  blocking collectives  71.5 us (11%)
  other arithmetic  48.3 us (7%)
  local copies, waits for them, and re-layouts  33.8 us (5%)
  between operations  13.6 us (2%)
    unnamed x2, waiting for transfers between devices  475 us
    all_gather x1, blocking collectives, shards(): piece = lax.all_gather(normed, 'chan', axis=0, tiled=True)  71.5 us
    scatter-add x1, other arithmetic, shards(): total = empty.at[labels].add(product, mode='drop')  44.9 us
    unnamed x261, local copies, waits for them, and re-layouts  21.8 us
  transfers between devices with their start and end apart: 1, of which 1 were waited for; matrix products, arithmetic and copies ran while one was open for 0% of the time, Pallas kernels for 0%

commit v1 on v0

--- a/solution.py
+++ b/solution.py
@@ -37,7 +37,9 @@
     first_row = lax.axis_index("chan") * chan_count
     own_rows = first_row + jnp.arange(chan_count, dtype=jnp.int32)[None, :]
     empty = jnp.zeros((bucket_count, LAGS), jnp.float32)
-    piece = lax.all_gather(normed, "chan", axis=0, tiled=True)
+    piece = jnp.concatenate(
+        lax.all_to_all(jnp.stack([normed] * lax.axis_size("chan")), "chan", 0, 0), axis=0
+    )
     row_count = piece.shape[0]
     product = jnp.dot(piece.reshape(row_count, -1), kernel, preferred_element_type=jnp.float32)
     product = product.reshape(row_count * chan_count, LAGS)

time: 648 us -> 596 us (0.920)
  blocking collectives: 71.5 us -> 0 us
  starting transfers between devices: 0.01 us -> 18.5 us
  waiting for transfers between devices: 475 us -> 468 us
    all_gather x1 -> x0, blocking collectives: 71.5 us -> none  [shards(): piece = lax.all_gather(normed, 'chan', axis=0, tiled=True)]
    all_to_all x0 -> x1, starting transfers between devices: none -> 18.5 us  [shards(): lax.all_to_all(jnp.stack([normed] * lax.axis_size('chan')), 'chan', 0, 0)]
    unnamed x261 -> x257, local copies, waits for them, and re-layouts: 21.8 us -> 21.7 us
  transfers between devices with their start and end apart: 1 -> 2, of which waited for: 1 -> 1; matrix products, arithmetic and copies ran while one was open for 0% -> 5% of each run, Pallas kernels for 0% -> 0%
where the time goes in v1:
time: 596 us; the launch traced here: 595 us
  waiting for transfers between devices  468 us (79%)
  other arithmetic  51 us (9%)
  local copies, waits for them, and re-layouts  37.6 us (6%)
  starting transfers between devices  18.5 us (3%)
  between operations  13.6 us (2%)
    unnamed x2, waiting for transfers between devices  468 us
    scatter-add x1, other arithmetic, shards(): total = empty.at[labels].add(product, mode='drop')  44.9 us
    unnamed x257, local copies, waits for them, and re-layouts  21.7 us
    all_to_all x1, starting transfers between devices, shards(): lax.all_to_all(jnp.stack([normed] * lax.axis_size('chan')), 'chan', 0, 0)  18.5 us
  transfers between devices with their start and end apart: 2, of which 1 were waited for; matrix products, arithmetic and copies ran while one was open for 5% of the time, Pallas kernels for 0%

profile of v1, /device:TPU:1, one launch (start us, length us, event | category | flops | bytes accessed | tf_op | source)
XLA Modules:
  0.0 594.8 jit_solution(4846320762757975763)
XLA Ops:
  6.5 0.9 fusion.5
  7.4 0.7 convert_element_type.26
  8.1 0.8 fusion.265
  8.9 0.8 stack.806
  9.7 18.5 %all-to-all-start = ((bf16[32,16,1,384]{3,1,2,0:T(8,128)(2,1)}), bf16[32,16,1,384]{3,1,2,0:T(8,128)(2,1)S(1)}, u32[]{:S(2)}, u32[]{:S(2)}) async-start(bf16[32,16,1,384]{3,1,2,0:T(8,128)(2,1)} %stack.806), calls=%async_computation | async-start | bytes 786432 | tf_op jit(solution)/shard_map/all_to_all | solution.py:41
  28.2 0.8 fusion.264
  29.5 0.1 constant_dynamic-update-slice_fusion.248
  29.6 0.1 constant_dynamic-update-slice_fusion.247
  29.7 0.1 constant_dynamic-update-slice_fusion.246
  29.8 0.1 constant_dynamic-update-slice_fusion.245
  30.4 0.1 constant_dynamic-update-slice_fusion.237
  30.5 0.1 constant_dynamic-update-slice_fusion.236
  30.6 0.1 constant_dynamic-update-slice_fusion.235
  30.7 0.1 constant_dynamic-update-slice_fusion.234
  30.7 0.1 constant_dynamic-update-slice_fusion.233
  30.8 0.1 constant_dynamic-update-slice_fusion.232
  30.9 0.1 constant_dynamic-update-slice_fusion.231
  31.0 0.1 constant_dynamic-update-slice_fusion.230
  31.1 0.1 constant_dynamic-update-slice_fusion.229
  31.1 0.1 constant_dynamic-update-slice_fusion.228
  31.2 0.1 constant_dynamic-update-slice_fusion.227
  31.3 0.1 constant_dynamic-update-slice_fusion.226
  32.0 0.1 constant_dynamic-update-slice_fusion.218
  32.0 0.1 constant_dynamic-update-slice_fusion.217
  32.1 0.1 constant_dynamic-update-slice_fusion.216
  32.2 0.1 constant_dynamic-update-slice_fusion.215
  32.3 0.1 constant_dynamic-update-slice_fusion.214
  32.4 0.1 constant_dynamic-update-slice_fusion.213
  32.4 0.1 constant_dynamic-update-slice_fusion.212
  32.5 0.1 constant_dynamic-update-slice_fusion.211
  32.6 0.1 constant_dynamic-update-slice_fusion.210
  32.7 0.1 constant_dynamic-update-slice_fusion.209
  32.8 0.1 constant_dynamic-update-slice_fusion.208
  32.9 0.1 constant_dynamic-update-slice_fusion.207
  33.5 0.1 constant_dynamic-update-slice_fusion.199
  33.6 0.1 constant_dynamic-update-slice_fusion.198
  33.7 0.1 constant_dynamic-update-slice_fusion.197
  33.8 0.1 constant_dynamic-update-slice_fusion.196
  33.8 0.1 constant_dynamic-update-slice_fusion.195
  33.9 0.1 constant_dynamic-update-slice_fusion.194
  34.0 0.1 constant_dynamic-update-slice_fusion.193
  34.1 0.1 constant_dynamic-update-slice_fusion.192
  34.2 0.1 constant_dynamic-update-slice_fusion.191
  34.2 0.1 constant_dynamic-update-slice_fusion.190
  34.3 0.1 constant_dynamic-update-slice_fusion.189
  34.4 0.1 constant_dynamic-update-slice_fusion.188
  35.1 0.1 constant_dynamic-update-slice_fusion.180
  35.1 0.1 constant_dynamic-update-slice_fusion.179
  35.2 0.1 constant_dynamic-update-slice_fusion.178
  35.3 0.1 constant_dynamic-update-slice_fusion.177
  35.4 0.1 constant_dynamic-update-slice_fusion.176
  39.4 0.1 constant_dynamic-update-slice_fusion.127
  49.8 0.8 copy.264
  50.6 1.4 bitcast_select_fusion
  52.1 1.6 copy.263
  53.7 1.7 reshape.163
  55.4 1.4 compare_select_fusion
  56.7 5.6 fusion.261
  62.3 9.3 %reshape.171 = f32[8192,256]{1,0:T(8,128)} reshape(f32[512,4096]{1,0:T(8,128)} %fusion.261) | data formatting | bytes 16777216 | tf_op jit(solution)/shard_map/reshape | solution.py:45
  71.6 44.9 %scatter_custom_fusion = f32[1024,256]{1,0:T(8,128)S(1)} fusion(s32[8192]{0:T(1024)} %bitcast.1036, f32[8192,256]{1,0:T(8,128)} %reshape.171, f32[]{:T(128)} %constant.13.clone.1), kind=kCustom, calls=%fused_computation.258 | custom fusion | flops 2097152 | bytes 1049088 | tf_op jit(solution)/shard_map/scatter-add | solution.py:49
  116.5 0.1 broadcast_multiply_fusion
  116.6 1.7 reshape.166
  118.3 468.4 %all-reduce.4.cloned.1.call-done = f32[512,2,256]{2,1,0:T(2,128)} async-done(((f32[512,2,256]{2,1,0:T(2,128)}), f32[512,2,256]{2,1,0:T(2,128)}) %all-reduce.4.cloned.1.call-update) | async-done | bytes 1048592
  586.7 1.2 constant_dynamic-slice_fusion
  (218 shorter events, 17.0 us)
Async XLA Ops:
  6.5 32.8 %copy-start = (bf16[16,1,384]{2,0,1:T(8,128)(2,1)S(1)}, bf16[16,1,384]{2,0,1:T(8,128)(2,1)}, u32[]{:S(2)}) copy-start(bf16[16,1,384]{2,0,1:T(8,128)(2,1)} %param.4) | copy-start | bytes 36868
  9.7 47.1 %all-to-all-start = ((bf16[32,16,1,384]{3,1,2,0:T(8,128)(2,1)}), bf16[32,16,1,384]{3,1,2,0:T(8,128)(2,1)S(1)}, u32[]{:S(2)}, u32[]{:S(2)}) async-start(bf16[32,16,1,384]{3,1,2,0:T(8,128)(2,1)} %stack.806), calls=%async_computation | async-start | bytes 786432 | tf_op jit(solution)/shard_map/all_to_all | solution.py:41
  28.2 558.5 %all-reduce.4.cloned.1.call-start = ((), (), s32[]{:S(2)}) async-start(), calls=%async_computation.1 | async-start | bytes 2097152
Sparse Core Ops, SparseCore 0:
  118.4 468.2 all-reduce.3
